TPU v7x, 256 devices: a whole 4x4x8 slice. The times are simulated.
256 devices in a mesh: group: 4 (over y), key: 64 (over z, x, core).
Axes of the slice: x: 4, y: 4, z: 8, core: 2. Of those that a mesh axis runs over, the one named last changes fastest.
Arguments:
- src_desc: bfloat16 [65536, 256], P(('group', 'key'))
- tgt_desc: bfloat16 [131072, 256], P('key')
- src_weight: float32 [65536], P(('group', 'key')), may hold values from 0.05 to 20
- tgt_weight: float32 [131072], P('key'), may hold values from 0.05 to 20
- tgt_dual: float32 [131072], P('key'), may hold values from -1.2 to 1.2
- pair_blocks: int32 [4, 64, 2, 64], P('group', 'key'), may hold values from 0 to 63, as said below
- pair_count: int32 [4, 64], P('group', 'key'), may hold values from 8 to 64, as said below
Outputs:
- src_dual: float32 [65536], P(('group', 'key'))
- tgt_dual_new: float32 [131072], P('key')
Inputs may be any that keep to these rules, and one draw needn't show every extreme that they name: `pair_blocks`: row 0 holds source clusters 0 to 63, row 1 target clusters 0 to 7; the live slots of one device are distinct pairs; every source cluster and every target cluster is in some live pair. `pair_count`: live slots come first.
All inputs are finite; a program needn't handle non-finite values.
Results may differ from a plain program's by a relative error of at most 0.0003.
Values may be sent and summed in bfloat16 or wider, within the bound.
No kernel may reach another device: no remote copies, remote signals or barrier semaphores. Data moves between devices by JAX's collectives and lax.ppermute only.
A program may use at most 64 MiB of HBM per device.

v0:
```python
import jax
import jax.numpy as jnp
from jax import lax
from jax.sharding import PartitionSpec as P

CLUSTER = 256


ENTROPY = 0.05
NEG_FLOOR = -1e30


def joined(value, axis, join):
    pieces = jax.tree.map(lambda part: lax.all_gather(part, axis), value)
    head = jax.tree.map(lambda part: part[0], pieces)
    tail = jax.tree.map(lambda part: part[1:], pieces)
    subtotal, _ = lax.scan(lambda subtotal, piece: (join(subtotal, piece), None), head, tail)
    return subtotal


def combine_pairs(first, second):
    top = jnp.maximum(first[0], second[0])
    total = first[1] * jnp.exp(first[0] - top) + second[1] * jnp.exp(second[0] - top)
    return (top, total)


def row_update(tops, totals, cluster_id, scores, reduce_axis):
    peak = jnp.max(scores, axis=reduce_axis)
    old_top = lax.dynamic_index_in_dim(tops, cluster_id, 0, keepdims=False)
    old_total = lax.dynamic_index_in_dim(totals, cluster_id, 0, keepdims=False)
    new_top = jnp.maximum(old_top, peak)
    shifted = scores - jnp.expand_dims(new_top, reduce_axis)
    new_total = old_total * jnp.exp(old_top - new_top) + jnp.sum(jnp.exp(shifted), axis=reduce_axis)
    tops = lax.dynamic_update_index_in_dim(tops, new_top, cluster_id, 0)
    totals = lax.dynamic_update_index_in_dim(totals, new_total, cluster_id, 0)
    return (tops, totals)


def local(src_desc, tgt_desc, src_weight, tgt_weight, tgt_dual, pair_blocks, pair_count):
    feature_width = src_desc.shape[1]
    own_clusters = src_desc.shape[0] // CLUSTER
    src_clusters = own_clusters * lax.axis_size("key")
    tgt_clusters = tgt_desc.shape[0] // CLUSTER
    slot_total = pair_blocks.shape[3]
    slot_ids = pair_blocks.reshape(2, slot_total)
    pair_total = pair_count.reshape(())
    sq_tgt = jnp.sum(tgt_desc.astype(jnp.float32) ** 2, axis=1) / feature_width

    def first_scores(slot, cost):
        tgt_pot = lax.dynamic_slice_in_dim(tgt_dual, slot_ids[1, slot] * CLUSTER, CLUSTER, 0)
        return (tgt_pot[None, :] - cost) / ENTROPY

    src_tops = jnp.full((src_clusters, CLUSTER), NEG_FLOOR, jnp.float32)
    src_totals = jnp.zeros((src_clusters, CLUSTER), jnp.float32)
    group_src = lax.all_gather(src_desc, "key", axis=0, tiled=True)
    sq_src = jnp.sum(group_src.astype(jnp.float32) ** 2, axis=1) / feature_width

    def block_cost(src_id, tgt_id):
        src_rows = lax.dynamic_slice_in_dim(group_src, src_id * CLUSTER, CLUSTER, 0)
        tgt_rows = lax.dynamic_slice_in_dim(tgt_desc, tgt_id * CLUSTER, CLUSTER, 0)
        inner = lax.dot_general(
            src_rows, tgt_rows, (((1,), (1,)), ((), ())), preferred_element_type=jnp.float32
        )
        src_sq = lax.dynamic_slice_in_dim(sq_src, src_id * CLUSTER, CLUSTER, 0)
        tgt_sq = lax.dynamic_slice_in_dim(sq_tgt, tgt_id * CLUSTER, CLUSTER, 0)
        return src_sq[:, None] + tgt_sq[None, :] - 2.0 / feature_width * inner

    def first_again(slot, carry):
        cost = block_cost(slot_ids[0, slot], slot_ids[1, slot])
        return row_update(carry[0], carry[1], slot_ids[0, slot], first_scores(slot, cost), 1)

    src_tops, src_totals = lax.fori_loop(0, pair_total, first_again, (src_tops, src_totals))

    def second_cost(slot):
        return block_cost(slot_ids[0, slot], slot_ids[1, slot])

    share_start = lax.axis_index("key") * own_clusters
    full_top, full_total = joined((src_tops, src_totals), "key", combine_pairs)
    share_top = lax.dynamic_slice_in_dim(full_top, share_start, own_clusters, 0)
    share_total = lax.dynamic_slice_in_dim(full_total, share_start, own_clusters, 0)
    share_lse = (share_top + jnp.log(share_total)).reshape(-1)
    src_dual = ENTROPY * jnp.log(src_weight) - ENTROPY * share_lse
    group_dual = lax.all_gather(src_dual, "key", axis=0, tiled=True)
    tgt_tops = jnp.full((tgt_clusters, CLUSTER), NEG_FLOOR, jnp.float32)
    tgt_totals = jnp.zeros((tgt_clusters, CLUSTER), jnp.float32)

    def second_step(slot, carry):
        src_pot = lax.dynamic_slice_in_dim(group_dual, slot_ids[0, slot] * CLUSTER, CLUSTER, 0)
        scores = (src_pot[:, None] - second_cost(slot)) / ENTROPY
        return row_update(carry[0], carry[1], slot_ids[1, slot], scores, 0)

    tgt_tops, tgt_totals = lax.fori_loop(0, pair_total, second_step, (tgt_tops, tgt_totals))
    merged_top, merged_total = joined((tgt_tops, tgt_totals), "group", combine_pairs)
    tgt_lse = (merged_top + jnp.log(merged_total)).reshape(-1)
    tgt_dual_new = ENTROPY * jnp.log(tgt_weight) - ENTROPY * tgt_lse
    return (src_dual, tgt_dual_new)


def solution(mesh):
    in_specs = (
        P(("group", "key"), None),
        P("key", None),
        P(("group", "key")),
        P("key"),
        P("key"),
        P("group", "key", None, None),
        P("group", "key"),
    )
    out_specs = (P(("group", "key")), P("key"))
    return jax.shard_map(local, mesh=mesh, in_specs=in_specs, out_specs=out_specs, check_vma=False)
```

profile of v0, /device:TPU:78, one launch (start us, length us, event | category | flops | bytes accessed | tf_op | source)
XLA Modules:
  0.0 1238.8 jit_solution(8359341190646817518)
XLA Ops:
  8.0 1.6 multiply_reduce_fusion.1
  9.5 82.9 %all-gather.9.cloned.1.call-done = bf16[16384,256]{1,0:T(8,128)(2,1)} async-done(((bf16[256,256]{1,0:T(8,128)(2,1)}), bf16[16384,256]{1,0:T(8,128)(2,1)}) %all-gather.9.cloned.1.call-update) | async-done | bytes 8388624 | tf_op jit(solution)/shard_map/all_gather | solution.py:55
  92.5 5.2 multiply_reduce_fusion
  97.7 55.6 %while.48 = (s32[]{:T(128)}, f32[64,256]{1,0:T(8,128)S(1)}, f32[64,256]{1,0:T(8,128)S(1)}, s32[]{:T(128)}, s32[2,64]{1,0:T(2,128)S(1)}, /*index=5*/f32[2048]{0:T...) while((s32[]{:T(128)}, f32[64,256]{1,0:T(8,128)S(1)}, ...), condition=%wide.region_5.6_spmd, body=%wide.region_2.5_spmd.sunk | while | flops 34079500 | bytes 814461 | solution.py:72
  103.2 1.2 fusion.30
  110.0 1.2 fusion.30
  116.9 1.2 fusion.30
  123.8 1.2 fusion.30
  130.6 1.2 fusion.30
  137.5 1.2 fusion.30
  144.4 1.2 fusion.30
  151.2 1.2 fusion.30
  154.7 457.8 %all-gather.11.cloned.1.call-done = f32[4096,256]{1,0:T(8,128)} async-done(((f32[64,256]{1,0:T(8,128)}), f32[4096,256]{1,0:T(8,128)}) %all-gather.11.cloned.1.call-update) | async-done | bytes 4194320 | tf_op jit(solution)/shard_map/all_gather | solution.py:14
  612.5 4.4 slice.42
  616.8 74.6 %all-gather.13.cloned.1.call-done = f32[4096,256]{1,0:T(8,128)} async-done(((f32[64,256]{1,0:T(8,128)}), f32[4096,256]{1,0:T(8,128)}) %all-gather.13.cloned.1.call-update) | async-done | bytes 4194320 | tf_op jit(solution)/shard_map/all_gather | solution.py:14
  691.4 4.4 slice.43
  695.8 60.1 %while.49 = (s32[]{:T(128)}, f32[64,256]{1,0:T(8,128)S(1)}, f32[64,256]{1,0:T(8,128)S(1)}, f32[63,64,256]{2,1,0:T(8,128)}, f32[63,64,256]{2,1,0:T(8,128)}, /*index=5*/s32[]{:T(128)}) while((s32[]{:T(128)}, f32[64,256]{1,0:T(8,128)S(1)}, f32[64,256]{1,0:T(8,128)S(1)}, f32[63,64,256]{2,1,0:T(8,128)}, f32[63,64,256]{2,1,0:T(8,128)}, ...), condition=%wide.region_7.8_spmd, body=%wide.region_6.7_spmd.sunk | while | flops 98306 | bytes 393297 | solution.py:17
  696.8 0.9 fusion.32
  697.7 0.9 fusion.32
  702.5 0.9 fusion.32
  756.0 42.6 %all-gather.4 = f32[64,1,256]{2,1,0:T(1,128)S(1)} all-gather(f32[1,1,256]{2,1,0:T(1,128)S(1)} %bitcast.83), channel_id=1, replica_groups=mesh['group'=4,'key'=64] {'key'}, dimensions={0}, use_global_device_ids=true | all-gather | bytes 66560 | tf_op jit(solution)/shard_map/all_gather | solution.py:83
  798.7 51.7 %while.50 = (s32[]{:T(128)}, f32[8,256]{1,0:T(8,128)S(1)}, f32[8,256]{1,0:T(8,128)S(1)}, s32[]{:T(128)}, s32[2,64]{1,0:T(2,128)S(1)}, /*index=5*/f32[16384]{0:T(...) while((s32[]{:T(128)}, f32[8,256]{1,0:T(8,128)S(1)}, ...), condition=%wide.region_11.12_spmd, body=%wide.region_8.11_spmd.sunk | while | flops 34079244 | bytes 811397 | solution.py:92
  803.6 1.2 fusion.33
  810.0 1.2 fusion.33
  816.4 1.2 fusion.33
  822.8 1.2 fusion.33
  829.1 1.2 fusion.33
  835.5 1.2 fusion.33
  841.9 1.2 fusion.33
  848.3 1.2 fusion.33
  850.4 369.2 %all-gather.3 = f32[32,256]{1,0:T(8,128)S(1)} all-gather(f32[8,256]{1,0:T(8,128)S(1)} %get-tuple-element.171), channel_id=5, replica_groups=mesh['group'=4,'key'=64] {'group'}, dimensions={0}, use_global_device_ids=true | all-gather | bytes 40960 | tf_op jit(solution)/shard_map/all_gather | solution.py:14
  1219.6 11.9 all-gather.2
  (253 shorter events, 82.0 us)
Async XLA Ops:
  7.2 90.6 %copy-start.2 = (s32[1,1,2,64]{3,2,1,0:T(2,128)S(1)}, s32[1,1,2,64]{3,2,1,0:T(2,128)}, u32[]{:S(2)}) copy-start(s32[1,1,2,64]{3,2,1,0:T(2,128)} %param.20) | copy-start | bytes 1540
  7.2 85.3 %all-gather.9.cloned.1.call-start = ((), (), s32[]{:S(2)}) async-start(), calls=%async_computation | async-start | bytes 8519680 | tf_op jit(solution)/shard_map/all_gather | solution.py:55
  7.9 604.5 %all-gather.11.cloned.1.call-start = ((), (), s32[]{:S(2)}) async-start(), calls=%async_computation.1 | async-start | bytes 4259840 | tf_op jit(solution)/shard_map/all_gather | solution.py:14
  153.3 0.6 copy-start
  153.3 0.7 copy-start.1
  153.9 537.5 %all-gather.13.cloned.1.call-start = ((), (), s32[]{:S(2)}) async-start(), calls=%async_computation.2 | async-start | bytes 4259840 | tf_op jit(solution)/shard_map/all_gather | solution.py:14
  612.5 83.4 %slice-start = ((f32[4096,256]{1,0:T(8,128)}), f32[64,256]{1,0:T(8,128)S(1)}, s32[]{:S(2)}) async-start(f32[4096,256]{1,0:T(8,128)} %all-gather.11.cloned.1.call-done), calls=%async_computation.3 | async-start | bytes 131072 | tf_op jit(solution)/shard_map/slice | solution.py:15
  612.5 143.6 %copy-start.5 = (f32[256]{0:T(256)S(1)}, f32[256]{0:T(256)}, u32[]{:S(2)}) copy-start(f32[256]{0:T(256)} %param.17) | copy-start | bytes 3076
  616.8 614.8 %copy-start.3 = (f32[2048]{0:T(1024)S(1)}, f32[2048]{0:T(1024)}, u32[]{:S(2)}) copy-start(f32[2048]{0:T(1024)} %param.18) | copy-start | bytes 24580
  691.4 4.4 slice-start.1
  756.0 476.2 %copy-start.4 = (f32[256]{0:T(256)}, f32[256]{0:T(256)S(1)}, u32[]{:S(2)}) copy-start(f32[256]{0:T(256)S(1)} %multiply_subtract_fusion.1) | copy-start | bytes 3076
Sparse Core Ops, SparseCore 0:
  10.7 81.6 all-gather.8
  154.1 458.3 all-gather.10
  615.2 76.1 all-gather.12
where the time goes:
time: 1250 us; the launch traced here: 1240 us
  waiting for transfers between devices  617 us (49%)
  blocking collectives  424 us (34%)
  other arithmetic  68.2 us (5%)
  loops' own time  66 us (5%)
  local copies, waits for them, and re-layouts  30.6 us (2%)
  matrix products  19.6 us (2%)
  between operations  13.9 us (1%)
    all_gather x2, waiting for transfers between devices, joined(): pieces = jax.tree.map(lambda part: lax.all_gather(part, axis), value)  532 us
    all_gather x2, blocking collectives, joined(): pieces = jax.tree.map(lambda part: lax.all_gather(part, axis), value)  381 us
    all_gather x1, waiting for transfers between devices, local(): group_src = lax.all_gather(src_desc, 'key', axis=0, tiled=True)  82.9 us
    add x66, other arithmetic, combine_pairs(): first[1] * jnp.exp(first[0] - top) + second[1] * jnp.exp(second[0] - top)  59.2 us
    all_gather x1, blocking collectives, local(): group_dual = lax.all_gather(src_dual, 'key', axis=0, tiled=True)  42.6 us
    another operation x1, loops' own time, local(): lax.fori_loop(0, pair_total, second_step, (tgt_tops, tgt_totals))  33.3 us
    another operation x1, loops' own time, local(): lax.fori_loop(0, pair_total, first_again, (src_tops, src_totals))  31.7 us
  transfers between devices with their start and end apart: 3, of which 3 were waited for; matrix products, arithmetic and copies ran while one was open for 0% of the time, Pallas kernels for 0%

commit v1 on v0

v1 whole, which is shorter than its diff:
```python
import functools

import jax
import jax.numpy as jnp
from jax import lax
from jax.experimental import pallas as pl
from jax.experimental.pallas import tpu as pltpu
from jax.sharding import PartitionSpec as P

CLUSTER = 256

ENTROPY = 0.05
INV_ENTROPY = 20.0
NEG_FLOOR = -1e30


def _slot_ids(ids_ref, slot, src_clusters, tgt_clusters):
    src_id = jnp.minimum(jnp.maximum(ids_ref[0, slot], 0), src_clusters - 1)
    tgt_id = jnp.minimum(jnp.maximum(ids_ref[1, slot], 0), tgt_clusters - 1)
    return src_id, tgt_id


def _block_cost(src_ref, tgt_ref, sqs_ref, sqt_ref, src_id, tgt_id, width):
    src_start = pl.multiple_of(src_id * CLUSTER, CLUSTER)
    tgt_start = pl.multiple_of(tgt_id * CLUSTER, CLUSTER)
    src_rows = src_ref[pl.ds(src_start, CLUSTER), :]
    tgt_rows = tgt_ref[pl.ds(tgt_start, CLUSTER), :]
    inner = lax.dot_general(
        tgt_rows, src_rows, (((1,), (1,)), ((), ())), preferred_element_type=jnp.float32
    )
    sq_s = sqs_ref[pl.ds(src_id, 1), :]
    sq_t = sqt_ref[pl.ds(tgt_start, CLUSTER), :]
    return (sq_s + sq_t) - (2.0 / width) * inner


def _first_kernel(ids_ref, cnt_ref, src_ref, tgt_ref, sqs_ref, sqt_ref, pot_ref, top_ref, tot_ref):
    src_clusters = sqs_ref.shape[0]
    tgt_clusters = tgt_ref.shape[0] // CLUSTER
    width = src_ref.shape[1]
    top_ref[...] = jnp.full(top_ref.shape, NEG_FLOOR, jnp.float32)
    tot_ref[...] = jnp.zeros(tot_ref.shape, jnp.float32)
    count = jnp.minimum(jnp.maximum(cnt_ref[0], 0), ids_ref.shape[1])

    def body(slot, carry):
        src_id, tgt_id = _slot_ids(ids_ref, slot, src_clusters, tgt_clusters)
        cost = _block_cost(src_ref, tgt_ref, sqs_ref, sqt_ref, src_id, tgt_id, width)
        pot = pot_ref[pl.ds(pl.multiple_of(tgt_id * CLUSTER, CLUSTER), CLUSTER), :]
        scores = (pot - cost) * INV_ENTROPY
        peak = jnp.max(scores, axis=0, keepdims=True)
        old_top = top_ref[pl.ds(src_id, 1), :]
        old_tot = tot_ref[pl.ds(src_id, 1), :]
        new_top = jnp.maximum(old_top, peak)
        new_tot = old_tot * jnp.exp(old_top - new_top) + jnp.sum(
            jnp.exp(scores - new_top), axis=0, keepdims=True
        )
        top_ref[pl.ds(src_id, 1), :] = new_top
        tot_ref[pl.ds(src_id, 1), :] = new_tot
        return carry

    lax.fori_loop(0, count, body, 0)


def _second_kernel(ids_ref, cnt_ref, src_ref, tgt_ref, sqs_ref, sqt_ref, dual_ref, top_ref, tot_ref):
    src_clusters = sqs_ref.shape[0]
    tgt_clusters = tgt_ref.shape[0] // CLUSTER
    width = src_ref.shape[1]
    top_ref[...] = jnp.full(top_ref.shape, NEG_FLOOR, jnp.float32)
    tot_ref[...] = jnp.zeros(tot_ref.shape, jnp.float32)
    count = jnp.minimum(jnp.maximum(cnt_ref[0], 0), ids_ref.shape[1])

    def body(slot, carry):
        src_id, tgt_id = _slot_ids(ids_ref, slot, src_clusters, tgt_clusters)
        cost = _block_cost(src_ref, tgt_ref, sqs_ref, sqt_ref, src_id, tgt_id, width)
        pot = dual_ref[pl.ds(src_id, 1), :]
        scores = (pot - cost) * INV_ENTROPY
        peak = jnp.max(scores, axis=1, keepdims=True)
        tgt_rows = pl.ds(pl.multiple_of(tgt_id * CLUSTER, CLUSTER), CLUSTER)
        old_top = top_ref[tgt_rows, :]
        old_tot = tot_ref[tgt_rows, :]
        new_top = jnp.maximum(old_top, peak)
        new_tot = old_tot * jnp.exp(old_top - new_top) + jnp.sum(
            jnp.exp(scores - new_top), axis=1, keepdims=True
        )
        top_ref[tgt_rows, :] = new_top
        tot_ref[tgt_rows, :] = new_tot
        return carry

    lax.fori_loop(0, count, body, 0)


def _sweep(kernel, out_shape, ids, cnt, group_src, tgt_desc, sq_src, sq_tgt, pot):
    vmem = pl.BlockSpec(memory_space=pltpu.VMEM)
    smem = pl.BlockSpec(memory_space=pltpu.SMEM)
    slots = ids.shape[1]
    flops = 2 * slots * CLUSTER * CLUSTER * group_src.shape[1]
    return pl.pallas_call(
        kernel,
        out_shape=(out_shape, out_shape),
        in_specs=[smem, smem, vmem, vmem, vmem, vmem, vmem],
        out_specs=(vmem, vmem),
        compiler_params=pltpu.CompilerParams(vmem_limit_bytes=48 * 1024 * 1024),
        cost_estimate=pl.CostEstimate(
            flops=flops,
            transcendentals=slots * CLUSTER * CLUSTER,
            bytes_accessed=group_src.size * 2 + tgt_desc.size * 2,
        ),
    )(ids, cnt, group_src, tgt_desc, sq_src, sq_tgt, pot)


def local(src_desc, tgt_desc, src_weight, tgt_weight, tgt_dual, pair_blocks, pair_count):
    width = src_desc.shape[1]
    own_clusters = src_desc.shape[0] // CLUSTER
    key_size = lax.axis_size("key")
    src_clusters = own_clusters * key_size
    tgt_clusters = tgt_desc.shape[0] // CLUSTER
    slot_total = pair_blocks.shape[3]
    ids = pair_blocks.reshape(2, slot_total)
    cnt = pair_count.reshape(1)

    sq_own = jnp.sum(src_desc.astype(jnp.float32) ** 2, axis=1) / width
    packed = jnp.stack([sq_own, src_weight]).reshape(2, own_clusters, CLUSTER)
    gathered = lax.all_gather(packed, "key", axis=1, tiled=True)
    sq_src = gathered[0]
    group_weight = gathered[1]
    group_src = lax.all_gather(src_desc, "key", axis=0, tiled=True)

    sq_tgt = (jnp.sum(tgt_desc.astype(jnp.float32) ** 2, axis=1) / width).reshape(-1, 1)
    pot_col = tgt_dual.reshape(-1, 1)

    src_shape = jax.ShapeDtypeStruct((src_clusters, CLUSTER), jnp.float32)
    src_tops, src_totals = _sweep(
        _first_kernel, src_shape, ids, cnt, group_src, tgt_desc, sq_src, sq_tgt, pot_col
    )
    full_top = lax.pmax(src_tops, "key")
    full_total = lax.psum(src_totals * jnp.exp(src_tops - full_top), "key")
    group_lse = full_top + jnp.log(full_total)
    group_dual = ENTROPY * jnp.log(group_weight) - ENTROPY * group_lse
    share_start = lax.axis_index("key") * own_clusters
    src_dual = lax.dynamic_slice_in_dim(group_dual, share_start, own_clusters, 0).reshape(-1)

    tgt_shape = jax.ShapeDtypeStruct((tgt_clusters * CLUSTER, 1), jnp.float32)
    tgt_tops, tgt_totals = _sweep(
        _second_kernel, tgt_shape, ids, cnt, group_src, tgt_desc, sq_src, sq_tgt, group_dual
    )
    tgt_pack = jnp.stack([tgt_tops.reshape(tgt_clusters, CLUSTER), tgt_totals.reshape(tgt_clusters, CLUSTER)])
    all_pack = lax.all_gather(tgt_pack, "group", axis=0)
    tops4 = all_pack[:, 0]
    tots4 = all_pack[:, 1]
    merged_top = jnp.max(tops4, axis=0)
    merged_total = jnp.sum(tots4 * jnp.exp(tops4 - merged_top[None]), axis=0)
    tgt_lse = (merged_top + jnp.log(merged_total)).reshape(-1)
    tgt_dual_new = ENTROPY * jnp.log(tgt_weight) - ENTROPY * tgt_lse
    return (src_dual, tgt_dual_new)


def solution(mesh):
    in_specs = (
        P(("group", "key"), None),
        P("key", None),
        P(("group", "key")),
        P("key"),
        P("key"),
        P("group", "key", None, None),
        P("group", "key"),
    )
    out_specs = (P(("group", "key")), P("key"))
    return jax.shard_map(local, mesh=mesh, in_specs=in_specs, out_specs=out_specs, check_vma=False)
```

time: 1250 us -> 514 us (0.41)
  the two profiles are of different devices: /device:TPU:78 before, /device:TPU:8 now
where the time goes in v1:
time: 514 us; the launch traced here: 504 us
  waiting for transfers between devices  380 us (74%)
  blocking collectives  72.8 us (14%)
  Pallas kernels  25.4 us (5%)
  between operations  14.6 us (3%)
  other arithmetic  8.7 us (2%)
    pmax x1, waiting for transfers between devices, local(): full_top = lax.pmax(src_tops, 'key')  179 us
    psum x1, waiting for transfers between devices, local(): full_total = lax.psum(src_totals * jnp.exp(src_tops - full_top), 'key')  170 us
    all_gather x1, blocking collectives, local(): gathered = lax.all_gather(packed, 'key', axis=1, tiled=True)  52.9 us
    all_gather x1, waiting for transfers between devices, local(): group_src = lax.all_gather(src_desc, 'key', axis=0, tiled=True)  30.5 us
    pallas_call x2, Pallas kernels, _sweep(): pl.pallas_call(kernel, out_shape=(out_shape, out_shape), in_specs=[smem,...  25.4 us
    all_gather x1, blocking collectives, local(): all_pack = lax.all_gather(tgt_pack, 'group', axis=0)  19.9 us
  transfers between devices with their start and end apart: 3, of which 3 were waited for; matrix products, arithmetic and copies ran while one was open for 1% of the time, Pallas kernels for 0%

profile of v1, /device:TPU:8, one launch (start us, length us, event | category | flops | bytes accessed | tf_op | source)
XLA Modules:
  0.0 504.0 jit_solution(10148326421336740782)
XLA Ops:
  7.2 0.0 copy-start
  7.2 0.0 copy-start.3
  7.2 0.0 copy-start.2
  7.2 0.0 all-gather.4.cloned.1.call-start
  7.2 0.7 all-gather.4.cloned.1.call-update
  7.9 0.0 all-reduce.3.cloned.1.call-start
  8.0 1.0 multiply_reduce_fusion.1
  9.0 0.7 pad_maximum_fusion.1
  9.7 52.9 %all-gather = f32[2,16384]{1,0:T(2,128)S(1)} all-gather(f32[2,256]{1,0:T(2,128)S(1)} %pad_maximum_fusion.1), channel_id=2, replica_groups=mesh['group'=4,'key'=64] {'key'}, dimensions={1}, use_global_device_ids=true | all-gather | bytes 133120 | tf_op jit(solution)/shard_map/all_gather | solution.py:122
  62.6 0.4 slice_reduce_fusion
  63.0 1.6 multiply_reduce_fusion
  64.7 0.4 copy.14.sqt_ref
  65.7 0.0 copy-done.3
  65.7 0.4 copy.15.pot_ref
  66.1 30.5 %all-gather.4.cloned.1.call-done.src_ref = bf16[16384,256]{1,0:T(8,128)(2,1)} async-done(((bf16[256,256]{1,0:T(8,128)(2,1)}), bf16[16384,256]{1,0:T(8,128)(2,1)}) %all-gather.4.cloned.1.call-update) | async-done | bytes 8388624 | tf_op jit(solution)/shard_map/all_gather | solution.py:125
  96.6 0.0 copy-done
  96.6 0.0 copy-done.2
  96.6 11.0 %shard_map.86 = (f32[64,256]{1,0:T(8,128)}, f32[64,256]{1,0:T(8,128)S(1)}) custom-call(s32[2,64]{1,0:T(2,128)S(1)} %bitcast.28, s32[1]{0:T(128)} %bitcast.26.cnt_ref, bf16[16384,256]{1,0:T(8,128)(2,1)} %all-gather.4.cloned.1.call-done.src_ref, bf16[2048,256]{1,0:T(8,128)(2,1)S(1)} %copy-done, f32[64,256]{1,0:T(8,128)S(1)} %squeeze.10.sqs_ref, ...), custom_call_target="tpu_custom_call" | custom-call | flops 2147483648 | bytes 9437184 | tf_op jit(solution)/shard_map/pallas_call | solution.py:96
  107.7 0.0 all-reduce.3.cloned.1.call-update
  107.7 0.0 all-reduce.5.cloned.1.call-start
  107.7 179.1 %all-reduce.3.cloned.1.call-done = f32[64,256]{1,0:T(8,128)} async-done(((f32[64,256]{1,0:T(8,128)}), f32[64,256]{1,0:T(8,128)}) %all-reduce.3.cloned.1.call-update) | async-done | bytes 65552 | tf_op jit(solution)/shard_map/pmax | solution.py:134
  286.8 1.5 exponential_multiply_fusion
  288.4 0.0 all-reduce.5.cloned.1.call-update
  288.4 169.7 %all-reduce.5.cloned.1.call-done = f32[64,256]{1,0:T(8,128)} async-done(((f32[64,256]{1,0:T(8,128)}), f32[64,256]{1,0:T(8,128)}) %all-reduce.5.cloned.1.call-update) | async-done | bytes 65552 | tf_op jit(solution)/shard_map/psum | solution.py:135
  458.1 0.9 multiply_subtract_fusion.dual_ref
  459.0 14.3 %shard_map.87 = (f32[2048,1]{1,0:T(8,128)S(1)}, f32[2048,1]{1,0:T(8,128)S(1)}) custom-call(s32[2,64]{1,0:T(2,128)S(1)} %bitcast.29, s32[1]{0:T(128)} %bitcast.27.cnt_ref, bf16[16384,256]{1,0:T(8,128)(2,1)} %all-gather.4.cloned.1.call-done.src_ref, bf16[2048,256]{1,0:T(8,128)(2,1)S(1)} %copy-done, f32[64,256]{1,0:T(8,128)S(1)} %squeeze.10.sqs_ref, ...), custom_call_target="tpu_custom_call" | custom-call | flops 2147483648 | bytes 9437184 | tf_op jit(solution)/shard_map/pallas_call | solution.py:96
  473.4 1.0 copy-done.1
  474.4 1.6 reduce.3
  475.9 0.3 reduce.4
  476.3 19.9 %all-gather.1 = f32[8,8,256]{2,1,0:T(8,128)S(1)} all-gather(f32[2,8,256]{2,1,0:T(8,128)S(1)} %pad_maximum_fusion), channel_id=3, replica_groups=mesh['group'=4,'key'=64] {'group'}, dimensions={0}, use_global_device_ids=true | all-gather | bytes 81920 | tf_op jit(solution)/shard_map/all_gather | solution.py:146
  496.3 0.6 constant_dynamic-slice_fusion
  496.9 0.6 multiply_subtract_fusion.1
  (14 shorter events, 0.1 us)
Async XLA Ops:
  7.2 89.4 %copy-start = (bf16[2048,256]{1,0:T(8,128)(2,1)S(1)}, bf16[2048,256]{1,0:T(8,128)(2,1)}, u32[]{:S(2)}) copy-start(bf16[2048,256]{1,0:T(8,128)(2,1)} %tgt_ref.3) | copy-start | bytes 3145732
  7.2 58.5 %copy-start.3 = (f32[2048]{0:T(1024)S(1)}, f32[2048]{0:T(1024)}, u32[]{:S(2)}) copy-start(f32[2048]{0:T(1024)} %param.11) | copy-start | bytes 24580
  7.2 89.4 %copy-start.2 = (s32[1,1,2,64]{3,2,1,0:T(2,128)S(1)}, s32[1,1,2,64]{3,2,1,0:T(2,128)}, u32[]{:S(2)}) copy-start(s32[1,1,2,64]{3,2,1,0:T(2,128)} %param.12) | copy-start | bytes 1540
  7.2 89.4 %all-gather.4.cloned.1.call-start = ((), (), s32[]{:S(2)}) async-start(), calls=%async_computation | async-start | bytes 8519680 | tf_op jit(solution)/shard_map/all_gather | solution.py:125
  7.9 278.9 %all-reduce.3.cloned.1.call-start = ((), (), s32[]{:S(2)}) async-start(), calls=%async_computation.1 | async-start | bytes 131072 | tf_op jit(solution)/shard_map/pmax | solution.py:134
  107.7 350.4 %all-reduce.5.cloned.1.call-start = ((), (), s32[]{:S(2)}) async-start(), calls=%async_computation.2 | async-start | bytes 131072 | tf_op jit(solution)/shard_map/psum | solution.py:135
  473.4 1.0 copy-start.1
  474.4 22.5 %copy-start.4 = (f32[2048]{0:T(1024)S(1)}, f32[2048]{0:T(1024)}, u32[]{:S(2)}) copy-start(f32[2048]{0:T(1024)} %param.10) | copy-start | bytes 24580
Sparse Core Ops, SparseCore 0:
  10.8 85.7 all-gather.3
  107.8 179.0 all-reduce.2
  290.3 167.7 all-reduce.4

commit v2 on v1

--- a/solution.py
+++ b/solution.py
@@ -107,6 +107,25 @@
     )(ids, cnt, group_src, tgt_desc, sq_src, sq_tgt, pot)
 
 
+def merge(low, high):
+    top = jnp.maximum(low[0], high[0])
+    total = low[1] * jnp.exp(low[0] - top) + high[1] * jnp.exp(high[0] - top)
+    return jnp.concatenate([top[None], total[None], low[2:] + high[2:]], axis=0)
+
+
+def butterfly(planes, axis, size, index):
+    bit = 1
+    while bit < size:
+        perm = [(i, i ^ bit) for i in range(size)]
+        other = lax.ppermute(planes, axis, perm)
+        is_low = (index & bit) == 0
+        low = jnp.where(is_low, planes, other)
+        high = jnp.where(is_low, other, planes)
+        planes = merge(low, high)
+        bit *= 2
+    return planes
+
+
 def local(src_desc, tgt_desc, src_weight, tgt_weight, tgt_dual, pair_blocks, pair_count):
     width = src_desc.shape[1]
     own_clusters = src_desc.shape[0] // CLUSTER
@@ -117,12 +136,8 @@
     ids = pair_blocks.reshape(2, slot_total)
     cnt = pair_count.reshape(1)
 
-    sq_own = jnp.sum(src_desc.astype(jnp.float32) ** 2, axis=1) / width
-    packed = jnp.stack([sq_own, src_weight]).reshape(2, own_clusters, CLUSTER)
-    gathered = lax.all_gather(packed, "key", axis=1, tiled=True)
-    sq_src = gathered[0]
-    group_weight = gathered[1]
     group_src = lax.all_gather(src_desc, "key", axis=0, tiled=True)
+    sq_src = (jnp.sum(group_src.astype(jnp.float32) ** 2, axis=1) / width).reshape(src_clusters, CLUSTER)
 
     sq_tgt = (jnp.sum(tgt_desc.astype(jnp.float32) ** 2, axis=1) / width).reshape(-1, 1)
     pot_col = tgt_dual.reshape(-1, 1)
@@ -131,11 +146,16 @@
     src_tops, src_totals = _sweep(
         _first_kernel, src_shape, ids, cnt, group_src, tgt_desc, sq_src, sq_tgt, pot_col
     )
-    full_top = lax.pmax(src_tops, "key")
-    full_total = lax.psum(src_totals * jnp.exp(src_tops - full_top), "key")
+    key_index = lax.axis_index("key")
+    own_rows = lax.broadcasted_iota(jnp.int32, (src_clusters, CLUSTER), 0) // own_clusters == key_index
+    own_weight = jnp.tile(src_weight.reshape(own_clusters, CLUSTER), (key_size, 1))
+    weight_rows = jnp.where(own_rows, own_weight, jnp.zeros_like(own_weight))
+    full_top, full_total, group_weight = butterfly(
+        jnp.stack([src_tops, src_totals, weight_rows]), "key", key_size, key_index
+    )
     group_lse = full_top + jnp.log(full_total)
     group_dual = ENTROPY * jnp.log(group_weight) - ENTROPY * group_lse
-    share_start = lax.axis_index("key") * own_clusters
+    share_start = key_index * own_clusters
     src_dual = lax.dynamic_slice_in_dim(group_dual, share_start, own_clusters, 0).reshape(-1)
 
     tgt_shape = jax.ShapeDtypeStruct((tgt_clusters * CLUSTER, 1), jnp.float32)

time: 514 us -> 222 us (0.43); the launches traced: 504 us -> 220 us
  waiting for transfers between devices: 380 us -> 123 us
  blocking collectives: 72.8 us -> 28.8 us
  starting transfers between devices: 0.12 us -> 17.4 us
    pmax x1 -> x0, waiting for transfers between devices: 179 us -> none  [local(): full_top = lax.pmax(src_tops, 'key')]
    psum x1 -> x0, waiting for transfers between devices: 170 us -> none  [local(): full_total = lax.psum(src_totals * jnp.exp(src_tops - full_top), 'key')]
    all_gather x1, waiting for transfers between devices: 30.5 us -> 84.3 us  [local(): group_src = lax.all_gather(src_desc, 'key', axis=0, tiled=True)]
    all_gather x1 -> x0, blocking collectives: 52.9 us -> none  [local(): gathered = lax.all_gather(packed, 'key', axis=1, tiled=True)]
    ppermute x0 -> x6, waiting for transfers between devices: none -> 38 us  [butterfly(): other = lax.ppermute(planes, axis, perm)]
    ppermute x0 -> x6, starting transfers between devices: none -> 17.3 us  [butterfly(): other = lax.ppermute(planes, axis, perm)]
    all_gather x1, blocking collectives: 19.9 us -> 28.8 us  [local(): all_pack = lax.all_gather(tgt_pack, 'group', axis=0)]
  transfers between devices with their start and end apart: 3 -> 7, of which waited for: 3 -> 7; matrix products, arithmetic and copies ran while one was open for 1% -> 2% of each run, Pallas kernels for 0% -> 0%
where the time goes in v2:
time: 222 us; the launch traced here: 220 us
  waiting for transfers between devices  123 us (55%)
  blocking collectives  28.8 us (13%)
  Pallas kernels  22.4 us (10%)
  starting transfers between devices  17.4 us (8%)
  between operations  15 us (7%)
  other arithmetic  10.5 us (5%)
  local copies, waits for them, and re-layouts  3.01 us (1%)
    all_gather x1, waiting for transfers between devices, local(): group_src = lax.all_gather(src_desc, 'key', axis=0, tiled=True)  84.3 us
    ppermute x6, waiting for transfers between devices, butterfly(): other = lax.ppermute(planes, axis, perm)  38 us
    all_gather x1, blocking collectives, local(): all_pack = lax.all_gather(tgt_pack, 'group', axis=0)  28.8 us
    pallas_call x2, Pallas kernels, _sweep(): pl.pallas_call(kernel, out_shape=(out_shape, out_shape), in_specs=[smem,...  22.4 us
    ppermute x6, starting transfers between devices, butterfly(): other = lax.ppermute(planes, axis, perm)  17.3 us
    reduce_sum x1, other arithmetic, local(): jnp.sum(group_src.astype(jnp.float32) ** 2, axis=1) / width  5.21 us
  transfers between devices with their start and end apart: 7, of which 7 were waited for; matrix products, arithmetic and copies ran while one was open for 2% of the time, Pallas kernels for 0%

profile of v2, /device:TPU:8, one launch (start us, length us, event | category | flops | bytes accessed | tf_op | source)
XLA Modules:
  0.0 220.2 jit_solution(7059728257669133858)
XLA Ops:
  7.2 0.0 copy-start
  7.2 0.0 copy-start.2
  7.2 0.0 all-gather.3.cloned.1.call-start
  7.2 0.7 all-gather.3.cloned.1.call-update
  8.6 1.6 multiply_reduce_fusion.1
  10.2 0.4 copy.14.sqt_ref
  10.5 1.1 copy.15.pot_ref
  11.6 0.7 fusion.16
  12.3 84.3 %all-gather.3.cloned.1.call-done.src_ref = bf16[16384,256]{1,0:T(8,128)(2,1)} async-done(((bf16[256,256]{1,0:T(8,128)(2,1)}), bf16[16384,256]{1,0:T(8,128)(2,1)}) %all-gather.3.cloned.1.call-update) | async-done | bytes 8388624 | tf_op jit(solution)/shard_map/all_gather | solution.py:139
  96.6 5.2 %multiply_reduce_fusion = f32[16384]{0:T(1024)S(1)} fusion(bf16[16384,256]{1,0:T(8,128)(2,1)} %all-gather.3.cloned.1.call-done.src_ref), kind=kLoop, calls=%fused_computation | loop fusion | flops 12566528 | bytes 8454144 | tf_op jit(solution)/shard_map/reduce_sum | solution.py:140
  101.9 9.5 %shard_map.86 = (f32[64,256]{1,0:T(8,128)S(1)}, f32[64,256]{1,0:T(8,128)S(1)}) custom-call(s32[2,64]{1,0:T(2,128)S(1)} %bitcast.64, s32[1]{0:T(128)} %bitcast.58.cnt_ref, bf16[16384,256]{1,0:T(8,128)(2,1)} %all-gather.3.cloned.1.call-done.src_ref, bf16[2048,256]{1,0:T(8,128)(2,1)S(1)} %copy-done, f32[64,256]{1,0:T(8,128)S(1)} %div.23.sqs_ref, ...), custom_call_target="tpu_custom_call" | custom-call | flops 2147483648 | bytes 9437184 | tf_op jit(solution)/shard_map/pallas_call | solution.py:96
  111.4 0.1 collective-permute-start
  111.5 1.4 collective-permute-done
  113.1 10.0 %collective-permute-start.1 = (f32[3,64,256]{2,1,0:T(8,128)S(1)}, f32[3,64,256]{2,1,0:T(8,128)S(1)}, u32[]{:S(2)}, u32[]{:S(2)}) collective-permute-start(f32[3,64,256]{2,1,0:T(8,128)S(1)} %pad_maximum_fusion.1), channel_id=1, source_target_pairs={{0,2},{1,3},{2,0},{3,1},{4,6},{5,7},{6,4},{7,5},{8,10},{9,11},{10,... | collective-permute-start | bytes 589832 | tf_op jit(solution)/shard_map/ppermute | solution.py:120
  123.0 5.4 %collective-permute-done.1 = f32[3,64,256]{2,1,0:T(8,128)S(1)} collective-permute-done((f32[3,64,256]{2,1,0:T(8,128)S(1)}, f32[3,64,256]{2,1,0:T(8,128)S(1)}, u32[]{:S(2)}, u32[]{:S(2)}) %collective-permute-start.1) | collective-permute-done | bytes 196640 | tf_op jit(solution)/shard_map/ppermute | solution.py:120
  128.6 6.4 %collective-permute-start.2 = (f32[3,64,256]{2,1,0:T(8,128)S(1)}, f32[3,64,256]{2,1,0:T(8,128)S(1)}, u32[]{:S(2)}, u32[]{:S(2)}) collective-permute-start(f32[3,64,256]{2,1,0:T(8,128)S(1)} %pad_maximum_fusion.2), channel_id=1, source_target_pairs={{0,4},{1,5},{2,6},{3,7},{4,0},{5,1},{6,2},{7,3},{8,12},{9,13},{10,... | collective-permute-start | bytes 589832 | tf_op jit(solution)/shard_map/ppermute | solution.py:120
  135.0 4.6 %collective-permute-done.2 = f32[3,64,256]{2,1,0:T(8,128)S(1)} collective-permute-done((f32[3,64,256]{2,1,0:T(8,128)S(1)}, f32[3,64,256]{2,1,0:T(8,128)S(1)}, u32[]{:S(2)}, u32[]{:S(2)}) %collective-permute-start.2) | collective-permute-done | bytes 196640 | tf_op jit(solution)/shard_map/ppermute | solution.py:120
  139.6 0.7 collective-permute-start.3
  140.3 5.1 %collective-permute-done.3 = f32[3,64,256]{2,1,0:T(8,128)S(1)} collective-permute-done((f32[3,64,256]{2,1,0:T(8,128)S(1)}, f32[3,64,256]{2,1,0:T(8,128)S(1)}, u32[]{:S(2)}, u32[]{:S(2)}) %collective-permute-start.3) | collective-permute-done | bytes 196640 | tf_op jit(solution)/shard_map/ppermute | solution.py:120
  145.5 0.0 copy-start.3
  145.6 0.1 collective-permute-start.4
  145.7 10.0 %collective-permute-done.4 = f32[3,64,256]{2,1,0:T(8,128)S(1)} collective-permute-done((f32[3,64,256]{2,1,0:T(8,128)S(1)}, f32[3,64,256]{2,1,0:T(8,128)S(1)}, u32[]{:S(2)}, u32[]{:S(2)}) %collective-permute-start.4) | collective-permute-done | bytes 196640 | tf_op jit(solution)/shard_map/ppermute | solution.py:120
  155.8 0.1 collective-permute-start.5
  155.9 11.4 %collective-permute-done.5 = f32[3,64,256]{2,1,0:T(8,128)S(1)} collective-permute-done((f32[3,64,256]{2,1,0:T(8,128)S(1)}, f32[3,64,256]{2,1,0:T(8,128)S(1)}, u32[]{:S(2)}, u32[]{:S(2)}) %collective-permute-start.5) | collective-permute-done | bytes 196640 | tf_op jit(solution)/shard_map/ppermute | solution.py:120
  167.4 0.1 fusion.5.dual_ref
  167.4 0.6 constant_dynamic-slice_fusion
  168.0 12.9 %shard_map.87 = (f32[2048,1]{1,0:T(8,128)S(1)}, f32[2048,1]{1,0:T(8,128)S(1)}) custom-call(s32[2,64]{1,0:T(2,128)S(1)} %bitcast.65, s32[1]{0:T(128)} %bitcast.59.cnt_ref, bf16[16384,256]{1,0:T(8,128)(2,1)} %all-gather.3.cloned.1.call-done.src_ref, bf16[2048,256]{1,0:T(8,128)(2,1)S(1)} %copy-done, f32[64,256]{1,0:T(8,128)S(1)} %div.23.sqs_ref, ...), custom_call_target="tpu_custom_call" | custom-call | flops 2147483648 | bytes 9437184 | tf_op jit(solution)/shard_map/pallas_call | solution.py:96
  181.0 1.0 copy-done.1
  181.9 1.6 reduce.1
  183.5 0.3 reduce.2
  183.9 28.8 %all-gather = f32[8,8,256]{2,1,0:T(8,128)S(1)} all-gather(f32[2,8,256]{2,1,0:T(8,128)S(1)} %pad_maximum_fusion.6), channel_id=2, replica_groups=mesh['group'=4,'key'=64] {'group'}, dimensions={0}, use_global_device_ids=true | all-gather | bytes 81920 | tf_op jit(solution)/shard_map/all_gather | solution.py:166
  212.7 0.6 multiply_subtract_fusion
  (31 shorter events, 0.5 us)
Async XLA Ops:
  7.2 94.7 %copy-start = (bf16[2048,256]{1,0:T(8,128)(2,1)S(1)}, bf16[2048,256]{1,0:T(8,128)(2,1)}, u32[]{:S(2)}) copy-start(bf16[2048,256]{1,0:T(8,128)(2,1)} %tgt_ref.3) | copy-start | bytes 3145732
  7.2 94.7 %copy-start.2 = (s32[1,1,2,64]{3,2,1,0:T(2,128)S(1)}, s32[1,1,2,64]{3,2,1,0:T(2,128)}, u32[]{:S(2)}) copy-start(s32[1,1,2,64]{3,2,1,0:T(2,128)} %param.12) | copy-start | bytes 1540
  7.2 89.4 %all-gather.3.cloned.1.call-start = ((), (), s32[]{:S(2)}) async-start(), calls=%async_computation | async-start | bytes 8519680 | tf_op jit(solution)/shard_map/all_gather | solution.py:139
  111.4 1.5 collective-permute-start
  113.1 15.4 %collective-permute-start.1 = (f32[3,64,256]{2,1,0:T(8,128)S(1)}, f32[3,64,256]{2,1,0:T(8,128)S(1)}, u32[]{:S(2)}, u32[]{:S(2)}) collective-permute-start(f32[3,64,256]{2,1,0:T(8,128)S(1)} %pad_maximum_fusion.1), channel_id=1, source_target_pairs={{0,2},{1,3},{2,0},{3,1},{4,6},{5,7},{6,4},{7,5},{8,10},{9,11},{10,... | collective-permute-start | bytes 589832 | tf_op jit(solution)/shard_map/ppermute | solution.py:120
  128.6 11.0 %collective-permute-start.2 = (f32[3,64,256]{2,1,0:T(8,128)S(1)}, f32[3,64,256]{2,1,0:T(8,128)S(1)}, u32[]{:S(2)}, u32[]{:S(2)}) collective-permute-start(f32[3,64,256]{2,1,0:T(8,128)S(1)} %pad_maximum_fusion.2), channel_id=1, source_target_pairs={{0,4},{1,5},{2,6},{3,7},{4,0},{5,1},{6,2},{7,3},{8,12},{9,13},{10,... | collective-permute-start | bytes 589832 | tf_op jit(solution)/shard_map/ppermute | solution.py:120
  139.6 5.8 %collective-permute-start.3 = (f32[3,64,256]{2,1,0:T(8,128)S(1)}, f32[3,64,256]{2,1,0:T(8,128)S(1)}, u32[]{:S(2)}, u32[]{:S(2)}) collective-permute-start(f32[3,64,256]{2,1,0:T(8,128)S(1)} %pad_maximum_fusion.3), channel_id=1, source_target_pairs={{0,8},{1,9},{2,10},{3,11},{4,12},{5,13},{6,14},{7,15},{8,0},{9,1},... | collective-permute-start | bytes 589832 | tf_op jit(solution)/shard_map/ppermute | solution.py:120
  145.5 67.2 %copy-start.3 = (f32[2048]{0:T(1024)S(1)}, f32[2048]{0:T(1024)}, u32[]{:S(2)}) copy-start(f32[2048]{0:T(1024)} %param.10) | copy-start | bytes 24580
  145.6 10.1 %collective-permute-start.4 = (f32[3,64,256]{2,1,0:T(8,128)S(1)}, f32[3,64,256]{2,1,0:T(8,128)S(1)}, u32[]{:S(2)}, u32[]{:S(2)}) collective-permute-start(f32[3,64,256]{2,1,0:T(8,128)S(1)} %pad_maximum_fusion.4), channel_id=1, source_target_pairs={{0,16},{1,17},{2,18},{3,19},{4,20},{5,21},{6,22},{7,23},{8,24},{9,... | collective-permute-start | bytes 589832 | tf_op jit(solution)/shard_map/ppermute | solution.py:120
  155.8 11.5 %collective-permute-start.5 = (f32[3,64,256]{2,1,0:T(8,128)S(1)}, f32[3,64,256]{2,1,0:T(8,128)S(1)}, u32[]{:S(2)}, u32[]{:S(2)}) collective-permute-start(f32[3,64,256]{2,1,0:T(8,128)S(1)} %pad_maximum_fusion.5), channel_id=1, source_target_pairs={{0,32},{1,33},{2,34},{3,35},{4,36},{5,37},{6,38},{7,39},{8,40},{9,... | collective-permute-start | bytes 589832 | tf_op jit(solution)/shard_map/ppermute | solution.py:120
  181.0 1.0 copy-start.1
Sparse Core Ops, SparseCore 0:
  10.8 85.7 all-gather.2

commit v3 on v2

--- a/solution.py
+++ b/solution.py
@@ -8,10 +8,12 @@
 from jax.sharding import PartitionSpec as P
 
 CLUSTER = 256
+CORES = 2
 
 ENTROPY = 0.05
 INV_ENTROPY = 20.0
 NEG_FLOOR = -1e30
+KEY = ("chip", "core")
 
 
 def _slot_ids(ids_ref, slot, src_clusters, tgt_clusters):
@@ -20,15 +22,20 @@
     return src_id, tgt_id
 
 
+def _src_position(src_id, src_clusters):
+    return (src_id % CORES) * (src_clusters // CORES) + src_id // CORES
+
+
 def _block_cost(src_ref, tgt_ref, sqs_ref, sqt_ref, src_id, tgt_id, width):
-    src_start = pl.multiple_of(src_id * CLUSTER, CLUSTER)
+    src_pos = _src_position(src_id, sqs_ref.shape[0])
+    src_start = pl.multiple_of(src_pos * CLUSTER, CLUSTER)
     tgt_start = pl.multiple_of(tgt_id * CLUSTER, CLUSTER)
     src_rows = src_ref[pl.ds(src_start, CLUSTER), :]
     tgt_rows = tgt_ref[pl.ds(tgt_start, CLUSTER), :]
     inner = lax.dot_general(
         tgt_rows, src_rows, (((1,), (1,)), ((), ())), preferred_element_type=jnp.float32
     )
-    sq_s = sqs_ref[pl.ds(src_id, 1), :]
+    sq_s = sqs_ref[pl.ds(src_pos, 1), :]
     sq_t = sqt_ref[pl.ds(tgt_start, CLUSTER), :]
     return (sq_s + sq_t) - (2.0 / width) * inner
 
@@ -129,14 +136,15 @@
 def local(src_desc, tgt_desc, src_weight, tgt_weight, tgt_dual, pair_blocks, pair_count):
     width = src_desc.shape[1]
     own_clusters = src_desc.shape[0] // CLUSTER
-    key_size = lax.axis_size("key")
+    key_size = lax.axis_size(KEY)
     src_clusters = own_clusters * key_size
     tgt_clusters = tgt_desc.shape[0] // CLUSTER
     slot_total = pair_blocks.shape[3]
     ids = pair_blocks.reshape(2, slot_total)
     cnt = pair_count.reshape(1)
 
-    group_src = lax.all_gather(src_desc, "key", axis=0, tiled=True)
+    chip_src = lax.all_gather(src_desc, "chip", axis=0, tiled=True)
+    group_src = lax.all_gather(chip_src, "core", axis=0, tiled=True)
     sq_src = (jnp.sum(group_src.astype(jnp.float32) ** 2, axis=1) / width).reshape(src_clusters, CLUSTER)
 
     sq_tgt = (jnp.sum(tgt_desc.astype(jnp.float32) ** 2, axis=1) / width).reshape(-1, 1)
@@ -146,12 +154,12 @@
     src_tops, src_totals = _sweep(
         _first_kernel, src_shape, ids, cnt, group_src, tgt_desc, sq_src, sq_tgt, pot_col
     )
-    key_index = lax.axis_index("key")
+    key_index = lax.axis_index(KEY)
     own_rows = lax.broadcasted_iota(jnp.int32, (src_clusters, CLUSTER), 0) // own_clusters == key_index
     own_weight = jnp.tile(src_weight.reshape(own_clusters, CLUSTER), (key_size, 1))
     weight_rows = jnp.where(own_rows, own_weight, jnp.zeros_like(own_weight))
     full_top, full_total, group_weight = butterfly(
-        jnp.stack([src_tops, src_totals, weight_rows]), "key", key_size, key_index
+        jnp.stack([src_tops, src_totals, weight_rows]), KEY, key_size, key_index
     )
     group_lse = full_top + jnp.log(full_total)
     group_dual = ENTROPY * jnp.log(group_weight) - ENTROPY * group_lse
@@ -174,14 +182,16 @@
 
 
 def solution(mesh):
+    groups, keys = mesh.devices.shape
+    split = jax.sharding.Mesh(mesh.devices.reshape(groups, keys // CORES, CORES), ("group",) + KEY)
     in_specs = (
-        P(("group", "key"), None),
-        P("key", None),
-        P(("group", "key")),
-        P("key"),
-        P("key"),
-        P("group", "key", None, None),
-        P("group", "key"),
+        P(("group",) + KEY, None),
+        P(KEY, None),
+        P(("group",) + KEY),
+        P(KEY),
+        P(KEY),
+        P("group", KEY, None, None),
+        P("group", KEY),
     )
-    out_specs = (P(("group", "key")), P("key"))
-    return jax.shard_map(local, mesh=mesh, in_specs=in_specs, out_specs=out_specs, check_vma=False)
+    out_specs = (P(("group",) + KEY), P(KEY))
+    return jax.shard_map(local, mesh=split, in_specs=in_specs, out_specs=out_specs, check_vma=False)

time: 222 us -> 246 us (1.11)
  the two profiles are of different devices: /device:TPU:8 before, /device:TPU:2 now
where the time goes in v3:
time: 246 us; the launch traced here: 245 us
  waiting for transfers between devices  140 us (57%)
  blocking collectives  36.4 us (15%)
  starting transfers between devices  26.8 us (11%)
  between operations  15 us (6%)
  Pallas kernels  13.3 us (5%)
  other arithmetic  10.5 us (4%)
  local copies, waits for them, and re-layouts  3.01 us (1%)
    all_gather x1, waiting for transfers between devices, local(): chip_src = lax.all_gather(src_desc, 'chip', axis=0, tiled=True)  86.1 us
    all_gather x1, blocking collectives, local(): all_pack = lax.all_gather(tgt_pack, 'group', axis=0)  36.4 us
    ppermute x6, waiting for transfers between devices, butterfly(): other = lax.ppermute(planes, axis, perm)  32.4 us
    ppermute x6, starting transfers between devices, butterfly(): other = lax.ppermute(planes, axis, perm)  26.7 us
    all_gather x1, waiting for transfers between devices, local(): group_src = lax.all_gather(chip_src, 'core', axis=0, tiled=True)  20.6 us
    pallas_call x2, Pallas kernels, _sweep(): pl.pallas_call(kernel, out_shape=(out_shape, out_shape), in_specs=[smem,...  13.3 us
    reduce_sum x1, other arithmetic, local(): jnp.sum(group_src.astype(jnp.float32) ** 2, axis=1) / width  5.21 us
  transfers between devices with their start and end apart: 8, of which 8 were waited for; matrix products, arithmetic and copies ran while one was open for 2% of the time, Pallas kernels for 0%

profile of v3, /device:TPU:2, one launch (start us, length us, event | category | flops | bytes accessed | tf_op | source)
XLA Modules:
  0.0 244.8 jit_solution(13813322286278360692)
XLA Ops:
  7.2 0.0 all-gather.4.cloned.1.call-start
  7.2 0.7 all-gather.4.cloned.1.call-update
  7.9 0.0 all-gather.6.cloned.1.call-start
  8.0 86.1 %all-gather.4.cloned.1.call-done = bf16[8192,256]{1,0:T(8,128)(2,1)} async-done(((bf16[256,256]{1,0:T(8,128)(2,1)}), bf16[8192,256]{1,0:T(8,128)(2,1)}) %all-gather.4.cloned.1.call-update) | async-done | bytes 4194320 | tf_op jit(solution)/shard_map/all_gather | solution.py:146
  94.1 0.0 all-gather.6.cloned.1.call-update
  94.7 1.6 multiply_reduce_fusion.1
  96.3 0.4 copy.14.sqt_ref
  96.7 1.1 copy.15.pot_ref
  97.8 0.7 fusion.16
  98.5 20.6 %all-gather.6.cloned.1.call-done.src_ref = bf16[16384,256]{1,0:T(8,128)(2,1)} async-done(((bf16[8192,256]{1,0:T(8,128)(2,1)}), bf16[16384,256]{1,0:T(8,128)(2,1)}) %all-gather.6.cloned.1.call-update) | async-done | bytes 8388624 | tf_op jit(solution)/shard_map/all_gather | solution.py:147
  119.1 5.2 %multiply_reduce_fusion = f32[16384]{0:T(1024)S(1)} fusion(bf16[16384,256]{1,0:T(8,128)(2,1)} %all-gather.6.cloned.1.call-done.src_ref), kind=kLoop, calls=%fused_computation | loop fusion | flops 12566528 | bytes 8454144 | tf_op jit(solution)/shard_map/reduce_sum | solution.py:148
  124.4 5.9 %shard_map.86 = (f32[64,256]{1,0:T(8,128)S(1)}, f32[64,256]{1,0:T(8,128)S(1)}) custom-call(s32[2,64]{1,0:T(2,128)S(1)} %bitcast.64, s32[1]{0:T(128)} %bitcast.58.cnt_ref, bf16[16384,256]{1,0:T(8,128)(2,1)} %all-gather.6.cloned.1.call-done.src_ref, bf16[2048,256]{1,0:T(8,128)(2,1)S(1)} %copy-done, f32[64,256]{1,0:T(8,128)S(1)} %div.23.sqs_ref, ...), custom_call_target="tpu_custom_call" | custom-call | flops 2147483648 | bytes 9437184 | tf_op jit(solution)/shard_map/pallas_call | solution.py:103
  130.4 4.5 %collective-permute-start = (f32[3,64,256]{2,1,0:T(8,128)S(1)}, f32[3,64,256]{2,1,0:T(8,128)S(1)}, u32[]{:S(2)}, u32[]{:S(2)}) collective-permute-start(f32[3,64,256]{2,1,0:T(8,128)S(1)} %pad_maximum_fusion), channel_id=1, source_target_pairs={{0,1},{1,0},{2,3},{3,2},{4,5},{5,4},{6,7},{7,6},{8,9},{9,8},{10,11... | collective-permute-start | bytes 589832 | tf_op jit(solution)/shard_map/ppermute | solution.py:127
  134.9 1.1 collective-permute-done
  136.0 0.1 collective-permute-start.1
  136.1 7.2 %collective-permute-done.1 = f32[3,64,256]{2,1,0:T(8,128)S(1)} collective-permute-done((f32[3,64,256]{2,1,0:T(8,128)S(1)}, f32[3,64,256]{2,1,0:T(8,128)S(1)}, u32[]{:S(2)}, u32[]{:S(2)}) %collective-permute-start.1) | collective-permute-done | bytes 196640 | tf_op jit(solution)/shard_map/ppermute | solution.py:127
  143.4 7.4 %collective-permute-start.2 = (f32[3,64,256]{2,1,0:T(8,128)S(1)}, f32[3,64,256]{2,1,0:T(8,128)S(1)}, u32[]{:S(2)}, u32[]{:S(2)}) collective-permute-start(f32[3,64,256]{2,1,0:T(8,128)S(1)} %pad_maximum_fusion.2), channel_id=1, source_target_pairs={{0,4},{1,5},{2,6},{3,7},{4,0},{5,1},{6,2},{7,3},{8,12},{9,13},{10,... | collective-permute-start | bytes 589832 | tf_op jit(solution)/shard_map/ppermute | solution.py:127
  150.8 4.3 %collective-permute-done.2 = f32[3,64,256]{2,1,0:T(8,128)S(1)} collective-permute-done((f32[3,64,256]{2,1,0:T(8,128)S(1)}, f32[3,64,256]{2,1,0:T(8,128)S(1)}, u32[]{:S(2)}, u32[]{:S(2)}) %collective-permute-start.2) | collective-permute-done | bytes 196640 | tf_op jit(solution)/shard_map/ppermute | solution.py:127
  155.3 6.7 %collective-permute-start.3 = (f32[3,64,256]{2,1,0:T(8,128)S(1)}, f32[3,64,256]{2,1,0:T(8,128)S(1)}, u32[]{:S(2)}, u32[]{:S(2)}) collective-permute-start(f32[3,64,256]{2,1,0:T(8,128)S(1)} %pad_maximum_fusion.3), channel_id=1, source_target_pairs={{0,8},{1,9},{2,10},{3,11},{4,12},{5,13},{6,14},{7,15},{8,0},{9,1},... | collective-permute-start | bytes 589832 | tf_op jit(solution)/shard_map/ppermute | solution.py:127
  162.0 4.1 %collective-permute-done.3 = f32[3,64,256]{2,1,0:T(8,128)S(1)} collective-permute-done((f32[3,64,256]{2,1,0:T(8,128)S(1)}, f32[3,64,256]{2,1,0:T(8,128)S(1)}, u32[]{:S(2)}, u32[]{:S(2)}) %collective-permute-start.3) | collective-permute-done | bytes 196640 | tf_op jit(solution)/shard_map/ppermute | solution.py:127
  166.2 2.1 collective-permute-start.4
  168.3 8.3 %collective-permute-done.4 = f32[3,64,256]{2,1,0:T(8,128)S(1)} collective-permute-done((f32[3,64,256]{2,1,0:T(8,128)S(1)}, f32[3,64,256]{2,1,0:T(8,128)S(1)}, u32[]{:S(2)}, u32[]{:S(2)}) %collective-permute-start.4) | collective-permute-done | bytes 196640 | tf_op jit(solution)/shard_map/ppermute | solution.py:127
  176.7 5.9 %collective-permute-start.5 = (f32[3,64,256]{2,1,0:T(8,128)S(1)}, f32[3,64,256]{2,1,0:T(8,128)S(1)}, u32[]{:S(2)}, u32[]{:S(2)}) collective-permute-start(f32[3,64,256]{2,1,0:T(8,128)S(1)} %pad_maximum_fusion.5), channel_id=1, source_target_pairs={{0,32},{1,33},{2,34},{3,35},{4,36},{5,37},{6,38},{7,39},{8,40},{9,... | collective-permute-start | bytes 589832 | tf_op jit(solution)/shard_map/ppermute | solution.py:127
  182.6 7.4 %collective-permute-done.5 = f32[3,64,256]{2,1,0:T(8,128)S(1)} collective-permute-done((f32[3,64,256]{2,1,0:T(8,128)S(1)}, f32[3,64,256]{2,1,0:T(8,128)S(1)}, u32[]{:S(2)}, u32[]{:S(2)}) %collective-permute-start.5) | collective-permute-done | bytes 196640 | tf_op jit(solution)/shard_map/ppermute | solution.py:127
  190.0 0.1 fusion.5.dual_ref
  190.1 0.6 constant_dynamic-slice_fusion
  190.7 7.3 %shard_map.87 = (f32[2048,1]{1,0:T(8,128)S(1)}, f32[2048,1]{1,0:T(8,128)S(1)}) custom-call(s32[2,64]{1,0:T(2,128)S(1)} %bitcast.65, s32[1]{0:T(128)} %bitcast.59.cnt_ref, bf16[16384,256]{1,0:T(8,128)(2,1)} %all-gather.6.cloned.1.call-done.src_ref, bf16[2048,256]{1,0:T(8,128)(2,1)S(1)} %copy-done, f32[64,256]{1,0:T(8,128)S(1)} %div.23.sqs_ref, ...), custom_call_target="tpu_custom_call" | custom-call | flops 2147483648 | bytes 9437184 | tf_op jit(solution)/shard_map/pallas_call | solution.py:103
  198.0 1.0 copy-done.1
  199.0 1.6 reduce.1
  200.6 0.3 reduce.2
  200.9 36.4 %all-gather = f32[8,8,256]{2,1,0:T(8,128)S(1)} all-gather(f32[2,8,256]{2,1,0:T(8,128)S(1)} %pad_maximum_fusion.6), channel_id=2, replica_groups=mesh['group'=4,'chip'=32,'core'=2] {'group'}, dimensions={0}, use_global_device_ids=true | all-gather | bytes 81920 | tf_op jit(solution)/shard_map/all_gather | solution.py:174
  237.4 0.6 multiply_subtract_fusion
  (34 shorter events, 0.5 us)
Async XLA Ops:
  7.2 117.2 %copy-start = (bf16[2048,256]{1,0:T(8,128)(2,1)S(1)}, bf16[2048,256]{1,0:T(8,128)(2,1)}, u32[]{:S(2)}) copy-start(bf16[2048,256]{1,0:T(8,128)(2,1)} %tgt_ref.3) | copy-start | bytes 3145732
  7.2 117.2 %copy-start.2 = (s32[1,1,2,64]{3,2,1,0:T(2,128)S(1)}, s32[1,1,2,64]{3,2,1,0:T(2,128)}, u32[]{:S(2)}) copy-start(s32[1,1,2,64]{3,2,1,0:T(2,128)} %param.12) | copy-start | bytes 1540
  7.2 86.9 %all-gather.4.cloned.1.call-start = ((), (), s32[]{:S(2)}) async-start(), calls=%async_computation | async-start | bytes 4325376 | tf_op jit(solution)/shard_map/all_gather | solution.py:146
  7.9 111.2 %all-gather.6.cloned.1.call-start = ((), (), s32[]{:S(2)}) async-start(), calls=%async_computation.1 | async-start | bytes 12582912 | tf_op jit(solution)/shard_map/all_gather | solution.py:147
  130.4 5.6 %collective-permute-start = (f32[3,64,256]{2,1,0:T(8,128)S(1)}, f32[3,64,256]{2,1,0:T(8,128)S(1)}, u32[]{:S(2)}, u32[]{:S(2)}) collective-permute-start(f32[3,64,256]{2,1,0:T(8,128)S(1)} %pad_maximum_fusion), channel_id=1, source_target_pairs={{0,1},{1,0},{2,3},{3,2},{4,5},{5,4},{6,7},{7,6},{8,9},{9,8},{10,11... | collective-permute-start | bytes 589832 | tf_op jit(solution)/shard_map/ppermute | solution.py:127
  136.0 7.3 %collective-permute-start.1 = (f32[3,64,256]{2,1,0:T(8,128)S(1)}, f32[3,64,256]{2,1,0:T(8,128)S(1)}, u32[]{:S(2)}, u32[]{:S(2)}) collective-permute-start(f32[3,64,256]{2,1,0:T(8,128)S(1)} %pad_maximum_fusion.1), channel_id=1, source_target_pairs={{0,2},{1,3},{2,0},{3,1},{4,6},{5,7},{6,4},{7,5},{8,10},{9,11},{10,... | collective-permute-start | bytes 589832 | tf_op jit(solution)/shard_map/ppermute | solution.py:127
  143.4 11.8 %collective-permute-start.2 = (f32[3,64,256]{2,1,0:T(8,128)S(1)}, f32[3,64,256]{2,1,0:T(8,128)S(1)}, u32[]{:S(2)}, u32[]{:S(2)}) collective-permute-start(f32[3,64,256]{2,1,0:T(8,128)S(1)} %pad_maximum_fusion.2), channel_id=1, source_target_pairs={{0,4},{1,5},{2,6},{3,7},{4,0},{5,1},{6,2},{7,3},{8,12},{9,13},{10,... | collective-permute-start | bytes 589832 | tf_op jit(solution)/shard_map/ppermute | solution.py:127
  155.3 10.8 %collective-permute-start.3 = (f32[3,64,256]{2,1,0:T(8,128)S(1)}, f32[3,64,256]{2,1,0:T(8,128)S(1)}, u32[]{:S(2)}, u32[]{:S(2)}) collective-permute-start(f32[3,64,256]{2,1,0:T(8,128)S(1)} %pad_maximum_fusion.3), channel_id=1, source_target_pairs={{0,8},{1,9},{2,10},{3,11},{4,12},{5,13},{6,14},{7,15},{8,0},{9,1},... | collective-permute-start | bytes 589832 | tf_op jit(solution)/shard_map/ppermute | solution.py:127
  166.1 71.2 %copy-start.3 = (f32[2048]{0:T(1024)S(1)}, f32[2048]{0:T(1024)}, u32[]{:S(2)}) copy-start(f32[2048]{0:T(1024)} %param.10) | copy-start | bytes 24580
  166.2 10.4 %collective-permute-start.4 = (f32[3,64,256]{2,1,0:T(8,128)S(1)}, f32[3,64,256]{2,1,0:T(8,128)S(1)}, u32[]{:S(2)}, u32[]{:S(2)}) collective-permute-start(f32[3,64,256]{2,1,0:T(8,128)S(1)} %pad_maximum_fusion.4), channel_id=1, source_target_pairs={{0,16},{1,17},{2,18},{3,19},{4,20},{5,21},{6,22},{7,23},{8,24},{9,... | collective-permute-start | bytes 589832 | tf_op jit(solution)/shard_map/ppermute | solution.py:127
  176.7 13.3 %collective-permute-start.5 = (f32[3,64,256]{2,1,0:T(8,128)S(1)}, f32[3,64,256]{2,1,0:T(8,128)S(1)}, u32[]{:S(2)}, u32[]{:S(2)}) collective-permute-start(f32[3,64,256]{2,1,0:T(8,128)S(1)} %pad_maximum_fusion.5), channel_id=1, source_target_pairs={{0,32},{1,33},{2,34},{3,35},{4,36},{5,37},{6,38},{7,39},{8,40},{9,... | collective-permute-start | bytes 589832 | tf_op jit(solution)/shard_map/ppermute | solution.py:127
  198.0 1.0 copy-start.1
Sparse Core Ops, SparseCore 0:
  10.6 83.4 all-gather.3
  95.9 23.2 all-gather.5

commit v4 on v2

--- a/solution.py
+++ b/solution.py
@@ -41,11 +41,13 @@
     tot_ref[...] = jnp.zeros(tot_ref.shape, jnp.float32)
     count = jnp.minimum(jnp.maximum(cnt_ref[0], 0), ids_ref.shape[1])
 
-    def body(slot, carry):
+    def scores_of(slot):
         src_id, tgt_id = _slot_ids(ids_ref, slot, src_clusters, tgt_clusters)
         cost = _block_cost(src_ref, tgt_ref, sqs_ref, sqt_ref, src_id, tgt_id, width)
         pot = pot_ref[pl.ds(pl.multiple_of(tgt_id * CLUSTER, CLUSTER), CLUSTER), :]
-        scores = (pot - cost) * INV_ENTROPY
+        return src_id, (pot - cost) * INV_ENTROPY
+
+    def update(src_id, scores):
         peak = jnp.max(scores, axis=0, keepdims=True)
         old_top = top_ref[pl.ds(src_id, 1), :]
         old_tot = tot_ref[pl.ds(src_id, 1), :]
@@ -55,9 +57,19 @@
         )
         top_ref[pl.ds(src_id, 1), :] = new_top
         tot_ref[pl.ds(src_id, 1), :] = new_tot
+
+    def body(trip, carry):
+        first = scores_of(2 * trip)
+        second = scores_of(2 * trip + 1)
+        update(*first)
+        update(*second)
         return carry
 
-    lax.fori_loop(0, count, body, 0)
+    lax.fori_loop(0, count // 2, body, 0)
+
+    @pl.when(count % 2 == 1)
+    def _():
+        update(*scores_of(count - 1))
 
 
 def _second_kernel(ids_ref, cnt_ref, src_ref, tgt_ref, sqs_ref, sqt_ref, dual_ref, top_ref, tot_ref):
@@ -68,11 +80,13 @@
     tot_ref[...] = jnp.zeros(tot_ref.shape, jnp.float32)
     count = jnp.minimum(jnp.maximum(cnt_ref[0], 0), ids_ref.shape[1])
 
-    def body(slot, carry):
+    def scores_of(slot):
         src_id, tgt_id = _slot_ids(ids_ref, slot, src_clusters, tgt_clusters)
         cost = _block_cost(src_ref, tgt_ref, sqs_ref, sqt_ref, src_id, tgt_id, width)
         pot = dual_ref[pl.ds(src_id, 1), :]
-        scores = (pot - cost) * INV_ENTROPY
+        return tgt_id, (pot - cost) * INV_ENTROPY
+
+    def update(tgt_id, scores):
         peak = jnp.max(scores, axis=1, keepdims=True)
         tgt_rows = pl.ds(pl.multiple_of(tgt_id * CLUSTER, CLUSTER), CLUSTER)
         old_top = top_ref[tgt_rows, :]
@@ -83,9 +97,19 @@
         )
         top_ref[tgt_rows, :] = new_top
         tot_ref[tgt_rows, :] = new_tot
+
+    def body(trip, carry):
+        first = scores_of(2 * trip)
+        second = scores_of(2 * trip + 1)
+        update(*first)
+        update(*second)
         return carry
 
-    lax.fori_loop(0, count, body, 0)
+    lax.fori_loop(0, count // 2, body, 0)
+
+    @pl.when(count % 2 == 1)
+    def _():
+        update(*scores_of(count - 1))
 
 
 def _sweep(kernel, out_shape, ids, cnt, group_src, tgt_desc, sq_src, sq_tgt, pot):

time: 222 us -> 205 us (0.923); the launches traced: 220 us -> 206 us
  blocking collectives: 28.8 us -> 10.7 us
  Pallas kernels: 22.4 us -> 37.1 us
  starting transfers between devices: 17.4 us -> 3.63 us
  waiting for transfers between devices: 123 us -> 126 us
    all_gather x1, blocking collectives: 28.8 us -> 10.7 us  [local(): all_pack = lax.all_gather(tgt_pack, 'group', axis=0)]
    pallas_call x2, Pallas kernels: 22.4 us -> 37.1 us  [_sweep(): pl.pallas_call(kernel, out_shape=(out_shape, out_shape), in_specs=[smem,...]
    ppermute x6, starting transfers between devices: 17.3 us -> 3.59 us  [butterfly(): other = lax.ppermute(planes, axis, perm)]
    ppermute x6, waiting for transfers between devices: 38 us -> 41.1 us  [butterfly(): other = lax.ppermute(planes, axis, perm)]
where the time goes in v4:
time: 205 us; the launch traced here: 206 us
  waiting for transfers between devices  126 us (61%)
  Pallas kernels  37.1 us (18%)
  between operations  15 us (7%)
  blocking collectives  10.7 us (5%)
  other arithmetic  10.5 us (5%)
  starting transfers between devices  3.63 us (2%)
  local copies, waits for them, and re-layouts  3.01 us (1%)
    all_gather x1, waiting for transfers between devices, local(): group_src = lax.all_gather(src_desc, 'key', axis=0, tiled=True)  84.3 us
    ppermute x6, waiting for transfers between devices, butterfly(): other = lax.ppermute(planes, axis, perm)  41.1 us
    pallas_call x2, Pallas kernels, _sweep(): pl.pallas_call(kernel, out_shape=(out_shape, out_shape), in_specs=[smem,...  37.1 us
    all_gather x1, blocking collectives, local(): all_pack = lax.all_gather(tgt_pack, 'group', axis=0)  10.7 us
    reduce_sum x1, other arithmetic, local(): jnp.sum(group_src.astype(jnp.float32) ** 2, axis=1) / width  5.21 us
  transfers between devices with their start and end apart: 7, of which 7 were waited for; matrix products, arithmetic and copies ran while one was open for 2% of the time, Pallas kernels for 0%

profile of v4, /device:TPU:8, one launch (start us, length us, event | category | flops | bytes accessed | tf_op | source)
XLA Modules:
  0.0 206.0 jit_solution(88934932511406665)
XLA Ops:
  7.2 0.0 copy-start
  7.2 0.0 all-gather.3.cloned.1.call-start
  7.2 0.7 all-gather.3.cloned.1.call-update
  8.6 1.6 multiply_reduce_fusion.1
  10.2 0.4 copy.14.sqt_ref
  10.5 1.1 copy.15.pot_ref
  11.6 0.7 fusion.16
  12.3 84.3 %all-gather.3.cloned.1.call-done.src_ref = bf16[16384,256]{1,0:T(8,128)(2,1)} async-done(((bf16[256,256]{1,0:T(8,128)(2,1)}), bf16[16384,256]{1,0:T(8,128)(2,1)}) %all-gather.3.cloned.1.call-update) | async-done | bytes 8388624 | tf_op jit(solution)/shard_map/all_gather | solution.py:163
  96.6 5.2 %multiply_reduce_fusion = f32[16384]{0:T(1024)S(1)} fusion(bf16[16384,256]{1,0:T(8,128)(2,1)} %all-gather.3.cloned.1.call-done.src_ref), kind=kLoop, calls=%fused_computation | loop fusion | flops 12566528 | bytes 8454144 | tf_op jit(solution)/shard_map/reduce_sum | solution.py:164
  101.9 15.9 %shard_map.86 = (f32[64,256]{1,0:T(8,128)S(1)}, f32[64,256]{1,0:T(8,128)S(1)}) custom-call(s32[2,64]{1,0:T(2,128)S(1)} %bitcast.64, s32[1]{0:T(128)} %bitcast.58.cnt_ref, bf16[16384,256]{1,0:T(8,128)(2,1)} %all-gather.3.cloned.1.call-done.src_ref, bf16[2048,256]{1,0:T(8,128)(2,1)S(1)} %copy-done, f32[64,256]{1,0:T(8,128)S(1)} %div.23.sqs_ref, ...), custom_call_target="tpu_custom_call" | custom-call | flops 2147483648 | bytes 9437184 | tf_op jit(solution)/shard_map/pallas_call | solution.py:120
  117.8 0.1 collective-permute-start
  117.9 1.4 collective-permute-done
  119.4 0.1 collective-permute-start.1
  119.5 6.9 %collective-permute-done.1 = f32[3,64,256]{2,1,0:T(8,128)S(1)} collective-permute-done((f32[3,64,256]{2,1,0:T(8,128)S(1)}, f32[3,64,256]{2,1,0:T(8,128)S(1)}, u32[]{:S(2)}, u32[]{:S(2)}) %collective-permute-start.1) | collective-permute-done | bytes 196640 | tf_op jit(solution)/shard_map/ppermute | solution.py:144
  126.6 0.1 collective-permute-start.2
  126.7 7.6 %collective-permute-done.2 = f32[3,64,256]{2,1,0:T(8,128)S(1)} collective-permute-done((f32[3,64,256]{2,1,0:T(8,128)S(1)}, f32[3,64,256]{2,1,0:T(8,128)S(1)}, u32[]{:S(2)}, u32[]{:S(2)}) %collective-permute-start.2) | collective-permute-done | bytes 196640 | tf_op jit(solution)/shard_map/ppermute | solution.py:144
  134.3 0.1 collective-permute-start.3
  134.5 5.7 %collective-permute-done.3 = f32[3,64,256]{2,1,0:T(8,128)S(1)} collective-permute-done((f32[3,64,256]{2,1,0:T(8,128)S(1)}, f32[3,64,256]{2,1,0:T(8,128)S(1)}, u32[]{:S(2)}, u32[]{:S(2)}) %collective-permute-start.3) | collective-permute-done | bytes 196640 | tf_op jit(solution)/shard_map/ppermute | solution.py:144
  140.2 0.0 copy-start.3
  140.2 0.1 collective-permute-start.4
  140.3 8.9 %collective-permute-done.4 = f32[3,64,256]{2,1,0:T(8,128)S(1)} collective-permute-done((f32[3,64,256]{2,1,0:T(8,128)S(1)}, f32[3,64,256]{2,1,0:T(8,128)S(1)}, u32[]{:S(2)}, u32[]{:S(2)}) %collective-permute-start.4) | collective-permute-done | bytes 196640 | tf_op jit(solution)/shard_map/ppermute | solution.py:144
  149.3 3.1 %collective-permute-start.5 = (f32[3,64,256]{2,1,0:T(8,128)S(1)}, f32[3,64,256]{2,1,0:T(8,128)S(1)}, u32[]{:S(2)}, u32[]{:S(2)}) collective-permute-start(f32[3,64,256]{2,1,0:T(8,128)S(1)} %pad_maximum_fusion.5), channel_id=1, source_target_pairs={{0,32},{1,33},{2,34},{3,35},{4,36},{5,37},{6,38},{7,39},{8,40},{9,... | collective-permute-start | bytes 589832 | tf_op jit(solution)/shard_map/ppermute | solution.py:144
  152.5 10.6 %collective-permute-done.5 = f32[3,64,256]{2,1,0:T(8,128)S(1)} collective-permute-done((f32[3,64,256]{2,1,0:T(8,128)S(1)}, f32[3,64,256]{2,1,0:T(8,128)S(1)}, u32[]{:S(2)}, u32[]{:S(2)}) %collective-permute-start.5) | collective-permute-done | bytes 196640 | tf_op jit(solution)/shard_map/ppermute | solution.py:144
  163.1 0.1 fusion.5.dual_ref
  163.1 0.6 constant_dynamic-slice_fusion
  163.7 21.2 %shard_map.87 = (f32[2048,1]{1,0:T(8,128)S(1)}, f32[2048,1]{1,0:T(8,128)S(1)}) custom-call(s32[2,64]{1,0:T(2,128)S(1)} %bitcast.65, s32[1]{0:T(128)} %bitcast.59.cnt_ref, bf16[16384,256]{1,0:T(8,128)(2,1)} %all-gather.3.cloned.1.call-done.src_ref, bf16[2048,256]{1,0:T(8,128)(2,1)S(1)} %copy-done, f32[64,256]{1,0:T(8,128)S(1)} %div.23.sqs_ref, ...), custom_call_target="tpu_custom_call" | custom-call | flops 2147483648 | bytes 9437184 | tf_op jit(solution)/shard_map/pallas_call | solution.py:120
  184.9 1.0 copy-done.1
  185.9 1.6 reduce.1
  187.5 0.3 reduce.2
  187.8 10.7 %all-gather = f32[8,8,256]{2,1,0:T(8,128)S(1)} all-gather(f32[2,8,256]{2,1,0:T(8,128)S(1)} %pad_maximum_fusion.6), channel_id=2, replica_groups=mesh['group'=4,'key'=64] {'group'}, dimensions={0}, use_global_device_ids=true | all-gather | bytes 81920 | tf_op jit(solution)/shard_map/all_gather | solution.py:190
  198.6 0.0 copy-done.3
  198.6 0.6 multiply_subtract_fusion
  (31 shorter events, 0.5 us)
Async XLA Ops:
  7.2 94.7 %copy-start = (bf16[2048,256]{1,0:T(8,128)(2,1)S(1)}, bf16[2048,256]{1,0:T(8,128)(2,1)}, u32[]{:S(2)}) copy-start(bf16[2048,256]{1,0:T(8,128)(2,1)} %tgt_ref.3) | copy-start | bytes 3145732
  7.2 94.7 %copy-start.2 = (s32[1,1,2,64]{3,2,1,0:T(2,128)S(1)}, s32[1,1,2,64]{3,2,1,0:T(2,128)}, u32[]{:S(2)}) copy-start(s32[1,1,2,64]{3,2,1,0:T(2,128)} %param.12) | copy-start | bytes 1540
  7.2 89.4 %all-gather.3.cloned.1.call-start = ((), (), s32[]{:S(2)}) async-start(), calls=%async_computation | async-start | bytes 8519680 | tf_op jit(solution)/shard_map/all_gather | solution.py:163
  117.8 1.5 collective-permute-start
  119.4 7.0 %collective-permute-start.1 = (f32[3,64,256]{2,1,0:T(8,128)S(1)}, f32[3,64,256]{2,1,0:T(8,128)S(1)}, u32[]{:S(2)}, u32[]{:S(2)}) collective-permute-start(f32[3,64,256]{2,1,0:T(8,128)S(1)} %pad_maximum_fusion.1), channel_id=1, source_target_pairs={{0,2},{1,3},{2,0},{3,1},{4,6},{5,7},{6,4},{7,5},{8,10},{9,11},{10,... | collective-permute-start | bytes 589832 | tf_op jit(solution)/shard_map/ppermute | solution.py:144
  126.6 7.7 %collective-permute-start.2 = (f32[3,64,256]{2,1,0:T(8,128)S(1)}, f32[3,64,256]{2,1,0:T(8,128)S(1)}, u32[]{:S(2)}, u32[]{:S(2)}) collective-permute-start(f32[3,64,256]{2,1,0:T(8,128)S(1)} %pad_maximum_fusion.2), channel_id=1, source_target_pairs={{0,4},{1,5},{2,6},{3,7},{4,0},{5,1},{6,2},{7,3},{8,12},{9,13},{10,... | collective-permute-start | bytes 589832 | tf_op jit(solution)/shard_map/ppermute | solution.py:144
  134.3 5.8 %collective-permute-start.3 = (f32[3,64,256]{2,1,0:T(8,128)S(1)}, f32[3,64,256]{2,1,0:T(8,128)S(1)}, u32[]{:S(2)}, u32[]{:S(2)}) collective-permute-start(f32[3,64,256]{2,1,0:T(8,128)S(1)} %pad_maximum_fusion.3), channel_id=1, source_target_pairs={{0,8},{1,9},{2,10},{3,11},{4,12},{5,13},{6,14},{7,15},{8,0},{9,1},... | collective-permute-start | bytes 589832 | tf_op jit(solution)/shard_map/ppermute | solution.py:144
  140.2 58.4 %copy-start.3 = (f32[2048]{0:T(1024)S(1)}, f32[2048]{0:T(1024)}, u32[]{:S(2)}) copy-start(f32[2048]{0:T(1024)} %param.10) | copy-start | bytes 24580
  140.2 9.0 %collective-permute-start.4 = (f32[3,64,256]{2,1,0:T(8,128)S(1)}, f32[3,64,256]{2,1,0:T(8,128)S(1)}, u32[]{:S(2)}, u32[]{:S(2)}) collective-permute-start(f32[3,64,256]{2,1,0:T(8,128)S(1)} %pad_maximum_fusion.4), channel_id=1, source_target_pairs={{0,16},{1,17},{2,18},{3,19},{4,20},{5,21},{6,22},{7,23},{8,24},{9,... | collective-permute-start | bytes 589832 | tf_op jit(solution)/shard_map/ppermute | solution.py:144
  149.3 13.7 %collective-permute-start.5 = (f32[3,64,256]{2,1,0:T(8,128)S(1)}, f32[3,64,256]{2,1,0:T(8,128)S(1)}, u32[]{:S(2)}, u32[]{:S(2)}) collective-permute-start(f32[3,64,256]{2,1,0:T(8,128)S(1)} %pad_maximum_fusion.5), channel_id=1, source_target_pairs={{0,32},{1,33},{2,34},{3,35},{4,36},{5,37},{6,38},{7,39},{8,40},{9,... | collective-permute-start | bytes 589832 | tf_op jit(solution)/shard_map/ppermute | solution.py:144
  184.9 1.0 copy-start.1
Sparse Core Ops, SparseCore 0:
  10.8 85.7 all-gather.2
